TPU v7x, 512 devices: a whole 4x4x16 slice. The times are simulated.
512 devices in a mesh: gx: 32 (over z, core), gy: 16 (over x, y).
Axes of the slice: x: 4, y: 4, z: 16, core: 2. Of those that a mesh axis runs over, the one named last changes fastest.
Arguments:
- field: bfloat16 [1024, 65536], P('gx', 'gy'), may hold values from -6 to 6
- dw0: float32 [9, 32], replicated, may hold values from -2 to 2
- pw0: bfloat16 [32, 32], replicated, may hold values from -1.5 to 1.5
- dw1: float32 [9, 32], replicated, may hold values from -2 to 2
- pw1: bfloat16 [32, 64], replicated, may hold values from -1.5 to 1.5
- dw2: float32 [9, 64], replicated, may hold values from -2 to 2
- pw2: bfloat16 [64, 128], replicated, may hold values from -1 to 1
- dw3: float32 [9, 128], replicated, may hold values from -2 to 2
- pw3: bfloat16 [128, 256], replicated, may hold values from -0.75 to 0.75
- dw4: float32 [9, 256], replicated, may hold values from -2 to 2
- pw4: bfloat16 [256, 512], replicated, may hold values from -0.5 to 0.5
- dwc: float32 [4, 9, 512], replicated, may hold values from -2 to 2
- pwc: bfloat16 [4, 512, 512], replicated, may hold values from -0.375 to 0.375
Outputs:
- fine: bfloat16 [1024, 65536], P('gx', 'gy')
- coarse: bfloat16 [4, 4096], replicated
All inputs are finite; a program needn't handle non-finite values.
Results may differ from a plain program's by a relative error of at most 0.024.
Values may be sent and summed in bfloat16 or wider, within the bound.
No kernel may reach another device: no remote copies, remote signals or barrier semaphores. Data moves between devices by JAX's collectives and lax.ppermute only.
A program may use at most 64 MiB of HBM per device.

v0:
```python
import jax
import jax.numpy as jnp
from jax import lax
from jax.sharding import PartitionSpec as P

LC = 4


def shifted(value, axis, steps):
    count = lax.axis_size(axis)
    leading, last = (max(0, -steps), min(count, count - steps))
    return lax.ppermute(value, axis, [(source, source + steps) for source in range(leading, last)])


def padded_2(block, sides, width):
    for axis, dim in sides:
        count = lax.axis_size(axis)
        forward = [(i, i + 1) for i in range(count - 1)]
        backward = [(target, source) for source, target in forward]
        low = lax.ppermute(
            lax.slice_in_dim(block, block.shape[dim] - width, None, axis=dim), axis, forward
        )
        high = lax.ppermute(lax.slice_in_dim(block, 0, width, axis=dim), axis, backward)
        block = jnp.concatenate([low, block, high], axis=dim)
    return block


def gelu_tanh(value):
    return jax.nn.gelu(value, approximate=True)


def point_flat(spread, weight, rows, cols):
    chans = weight.shape[0]
    flat = spread.astype(jnp.bfloat16).reshape(rows * cols, chans)
    mixed = jnp.dot(flat, weight, preferred_element_type=jnp.float32)
    return gelu_tanh(mixed).reshape(rows, cols * weight.shape[1])


def down_level(field, taps, weight, split_rows, split_cols):
    chans = taps.shape[1]
    rows = field.shape[0]
    cols = field.shape[1] // chans
    half_rows = rows // 2
    half_cols = cols // 2
    if split_rows:
        upper = shifted(field[-1:], "gx", 1)
    else:
        upper = jnp.zeros((1, cols * chans), jnp.bfloat16)
    extended = jnp.concatenate([upper, field], axis=0)
    if split_cols:
        leftside = shifted(extended[:, -chans:], "gy", 1)
    else:
        leftside = jnp.zeros((rows + 1, chans), jnp.bfloat16)
    tiled = jnp.tile(taps, (1, half_cols))
    total = jnp.zeros((half_rows, half_cols * chans), jnp.float32)
    for first in range(3):
        slab = extended[first : first + rows : 2]
        left_slab = leftside[first : first + rows : 2]
        pairs = slab.reshape(half_rows, half_cols, 2 * chans)
        even_cells = pairs[:, :, :chans].reshape(half_rows, half_cols * chans)
        odd_cells = pairs[:, :, chans:].reshape(half_rows, half_cols * chans)
        before = jnp.concatenate([left_slab, odd_cells[:, :-chans]], axis=1)
        for second, piece in enumerate((before, even_cells, odd_cells)):
            total = total + piece.astype(jnp.float32) * tiled[3 * first + second]
    return point_flat(total, weight, half_rows, half_cols).astype(jnp.bfloat16)


def local(field, dw0, pw0, dw1, pw1, dw2, pw2, dw3, pw3, dw4, pw4, dwc, pwc):
    chans = dw0.shape[1]
    rows = field.shape[0]
    cols = field.shape[1] // chans
    grid = field.reshape(rows, cols, chans)
    padded = padded_2(grid, (("gx", 0), ("gy", 1)), 2)
    flat_pad = padded.reshape(rows + 4, (cols + 4) * chans)
    tiled = jnp.tile(dw0, (1, cols))
    total = jnp.zeros((rows, cols * chans), jnp.float32)
    for first in range(3):
        for second in range(3):
            piece = flat_pad[
                2 * first : 2 * first + rows, 2 * second * chans : 2 * second * chans + cols * chans
            ]
            total = total + piece.astype(jnp.float32) * tiled[3 * first + second]
    hidden = (field.astype(jnp.float32) + point_flat(total, pw0, rows, cols)).astype(jnp.bfloat16)
    fine = hidden
    for taps, weight in ((dw1, pw1), (dw2, pw2), (dw3, pw3), (dw4, pw4)):
        hidden = down_level(hidden, taps, weight, True, True)
    coarse_chans = dwc.shape[2]
    finished = 0
    for level in range(LC):
        if (
            finished == level
            and hidden.shape[0] % 2 == 0
            and (hidden.shape[1] // coarse_chans % 2 == 0)
        ):
            hidden = down_level(hidden, dwc[level], pwc[level], True, True)
            finished = level + 1
    hidden = lax.all_gather(hidden, "gx", axis=0, tiled=True)
    hidden = lax.all_gather(hidden, "gy", axis=1, tiled=True)
    for level in range(finished, LC):
        hidden = down_level(hidden, dwc[level], pwc[level], False, False)
    return (fine, hidden)


def solution(mesh):
    placed = (P("gx", "gy"), P(), P(), P(), P(), P(), P(), P(), P(), P(), P(), P(), P())
    return jax.shard_map(
        local, mesh=mesh, in_specs=placed, out_specs=(P("gx", "gy"), P()), check_vma=False
    )
```

profile of v0, /device:TPU:2, one launch (start us, length us, event | category | flops | bytes accessed | tf_op | source)
XLA Modules:
  0.0 278.6 jit_solution(14854291314269597330)
XLA Ops:
  8.3 1.7 collective-permute-start
  15.5 1.6 slice_bitcast_fusion.43
  17.1 1.6 fusion.201
  26.0 1.7 reshape.1235
  28.4 3.5 %collective-permute-start.2 = (bf16[36,2,32]{1,2,0:T(8,128)(2,1)S(1)}, bf16[36,2,32]{1,2,0:T(8,128)(2,1)S(1)}, u32[]{:S(2)}, u32[]{:S(2)}) collective-permute-start(bf16[36,2,32]{1,2,0:T(8,128)(2,1)S(1)} %get-tuple-element.8), channel_id=1, source_target_pairs={{0,1},{1,2},{2,3},{3,4},{4,5},{5,6},{6,7},{7,8},{8,9},{9,10},{10,1... | collective-permute-start | bytes 13832 | tf_op jit(solution)/shard_map/ppermute | solution.py:20
  31.9 4.5 %collective-permute-start.3 = (bf16[36,2,32]{1,2,0:T(8,128)(2,1)S(1)}, bf16[36,2,32]{1,2,0:T(8,128)(2,1)S(1)}, u32[]{:S(2)}, u32[]{:S(2)}) collective-permute-start(bf16[36,2,32]{1,2,0:T(8,128)(2,1)S(1)} %get-tuple-element.9), channel_id=1, source_target_pairs={{1,0},{2,1},{3,2},{4,3},{5,4},{6,5},{7,6},{8,7},{9,8},{10,9},{11,1... | collective-permute-start | bytes 13832 | tf_op jit(solution)/shard_map/ppermute | solution.py:23
  48.0 4.1 %collective-permute-start.4 = (bf16[1,4096]{1,0:T(2,128)(2,1)S(1)}, bf16[1,4096]{1,0:T(2,128)(2,1)S(1)}, u32[]{:S(2)}, u32[]{:S(2)}) collective-permute-start(bf16[1,4096]{1,0:T(2,128)(2,1)S(1)} %slice.1366), channel_id=1, source_target_pairs={{0,16},{16,32},{32,48},{48,64},{64,80},{80,96},{96,112},{112,128},... | collective-permute-start | bytes 24584 | tf_op jit(solution)/shard_map/ppermute | solution.py:12
  53.8 2.7 collective-permute-start.5
  57.3 4.2 %collective-permute-done.5 = bf16[33,32]{1,0:T(8,128)(2,1)S(1)} collective-permute-done((bf16[33,32]{1,0:T(8,128)(2,1)S(1)}, bf16[33,32]{1,0:T(8,128)(2,1)S(1)}, u32[]{:S(2)}, u32[]{:S(2)}) %collective-permute-start.5) | collective-permute-done | bytes 2144 | tf_op jit(solution)/shard_map/ppermute | solution.py:12
  64.8 4.7 %collective-permute-start.6 = (bf16[1,4096]{1,0:T(2,128)(2,1)S(1)}, bf16[1,4096]{1,0:T(2,128)(2,1)S(1)}, u32[]{:S(2)}, u32[]{:S(2)}) collective-permute-start(bf16[1,4096]{1,0:T(2,128)(2,1)S(1)} %slice.1129), channel_id=1, source_target_pairs={{0,16},{16,32},{32,48},{48,64},{64,80},{80,96},{96,112},{112,128},... | collective-permute-start | bytes 24584 | tf_op jit(solution)/shard_map/ppermute | solution.py:12
  70.5 1.9 collective-permute-start.7
  72.7 5.4 %collective-permute-done.7 = bf16[17,64]{1,0:T(8,128)(2,1)S(1)} collective-permute-done((bf16[17,64]{1,0:T(8,128)(2,1)S(1)}, bf16[17,64]{1,0:T(8,128)(2,1)S(1)}, u32[]{:S(2)}, u32[]{:S(2)}) %collective-permute-start.7) | collective-permute-done | bytes 2208 | tf_op jit(solution)/shard_map/ppermute | solution.py:12
  79.6 3.7 %collective-permute-start.8 = (bf16[1,4096]{1,0:T(2,128)(2,1)S(1)}, bf16[1,4096]{1,0:T(2,128)(2,1)S(1)}, u32[]{:S(2)}, u32[]{:S(2)}) collective-permute-start(bf16[1,4096]{1,0:T(2,128)(2,1)S(1)} %bitcast.639), channel_id=1, source_target_pairs={{0,16},{16,32},{32,48},{48,64},{64,80},{80,96},{96,112},{112,128},... | collective-permute-start | bytes 24584 | tf_op jit(solution)/shard_map/ppermute | solution.py:12
  84.1 1.9 collective-permute-start.9
  86.3 5.4 %collective-permute-done.9 = bf16[9,128]{1,0:T(8,128)(2,1)S(1)} collective-permute-done((bf16[9,128]{1,0:T(8,128)(2,1)S(1)}, bf16[9,128]{1,0:T(8,128)(2,1)S(1)}, u32[]{:S(2)}, u32[]{:S(2)}) %collective-permute-start.9) | collective-permute-done | bytes 2336 | tf_op jit(solution)/shard_map/ppermute | solution.py:12
  93.4 4.2 %collective-permute-start.10 = (bf16[1,4096]{1,0:T(2,128)(2,1)S(1)}, bf16[1,4096]{1,0:T(2,128)(2,1)S(1)}, u32[]{:S(2)}, u32[]{:S(2)}) collective-permute-start(bf16[1,4096]{1,0:T(2,128)(2,1)S(1)} %bitcast.640), channel_id=1, source_target_pairs={{0,16},{16,32},{32,48},{48,64},{64,80},{80,96},{96,112},{112,128},... | collective-permute-start | bytes 24584 | tf_op jit(solution)/shard_map/ppermute | solution.py:12
  98.6 1.9 collective-permute-start.11
  100.6 5.6 %collective-permute-done.11 = bf16[5,256]{1,0:T(8,128)(2,1)S(1)} collective-permute-done((bf16[5,256]{1,0:T(8,128)(2,1)S(1)}, bf16[5,256]{1,0:T(8,128)(2,1)S(1)}, u32[]{:S(2)}, u32[]{:S(2)}) %collective-permute-start.11) | collective-permute-done | bytes 2592 | tf_op jit(solution)/shard_map/ppermute | solution.py:12
  106.8 4.2 %collective-permute-start.12 = (bf16[1,4096]{1,0:T(2,128)(2,1)S(1)}, bf16[1,4096]{1,0:T(2,128)(2,1)S(1)}, u32[]{:S(2)}, u32[]{:S(2)}) collective-permute-start(bf16[1,4096]{1,0:T(2,128)(2,1)S(1)} %bitcast.638), channel_id=1, source_target_pairs={{0,16},{16,32},{32,48},{48,64},{64,80},{80,96},{96,112},{112,128},... | collective-permute-start | bytes 24584 | tf_op jit(solution)/shard_map/ppermute | solution.py:12
  111.9 1.9 collective-permute-start.13
  113.9 5.5 %collective-permute-done.13 = bf16[3,512]{1,0:T(4,128)(2,1)S(1)} collective-permute-done((bf16[3,512]{1,0:T(4,128)(2,1)S(1)}, bf16[3,512]{1,0:T(4,128)(2,1)S(1)}, u32[]{:S(2)}, u32[]{:S(2)}) %collective-permute-start.13) | collective-permute-done | bytes 3104 | tf_op jit(solution)/shard_map/ppermute | solution.py:12
  120.9 43.3 %all-gather = bf16[32,1,2048]{2,1,0:T(2,128)(2,1)S(1)} all-gather(bf16[1,1,2048]{2,1,0:T(2,128)(2,1)S(1)} %reshape.1338), channel_id=1, replica_groups=mesh['gx'=32,'gy'=16] {'gx'}, dimensions={0}, use_global_device_ids=true | all-gather | bytes 135168 | tf_op jit(solution)/shard_map/all_gather | solution.py:97
  180.3 41.1 %all-gather.3.cloned.1.call-done = bf16[32,32768]{1,0:T(8,128)(2,1)} async-done(((bf16[32,2048]{1,0:T(8,128)(2,1)}), bf16[32,32768]{1,0:T(8,128)(2,1)}) %all-gather.3.cloned.1.call-update) | async-done | bytes 2097168 | tf_op jit(solution)/shard_map/all_gather | solution.py:98
  221.4 1.8 concatenate.136
  223.2 7.5 %slice.1262 = bf16[16,32768]{1,0:T(8,128)(2,1)} slice(bf16[33,32768]{1,0:T(8,128)(2,1)S(1)} %concatenate.136), slice={[0:32:2], [0:32768:1]} | slice | bytes 2097152 | tf_op jit(solution)/shard_map/slice | solution.py:57
  230.7 1.8 copy.75
  235.4 7.5 %slice.1272 = bf16[16,32768]{1,0:T(8,128)(2,1)} slice(bf16[32,32768]{1,0:T(8,128)(2,1)S(1)} %copy-done.1), slice={[0:32:2], [0:32768:1]} | slice | bytes 2097152 | tf_op jit(solution)/shard_map/slice | solution.py:57
  242.9 1.8 copy.81
  244.9 1.6 copy.84
  246.5 7.5 %slice.1282 = bf16[16,32768]{1,0:T(8,128)(2,1)} slice(bf16[32,32768]{1,0:T(8,128)(2,1)S(1)} %copy-done.1), slice={[1:32:2], [0:32768:1]} | slice | bytes 2097152 | tf_op jit(solution)/shard_map/slice | solution.py:57
  253.9 1.8 copy.87
  259.4 1.7 fusion.7
  (505 shorter events, 72.4 us)
Async XLA Ops:
  7.2 99.3 %copy-start = (bf16[256,512]{1,0:T(8,128)(2,1)S(1)}, bf16[256,512]{1,0:T(8,128)(2,1)}, u32[]{:S(2)}) copy-start(bf16[256,512]{1,0:T(8,128)(2,1)} %param.23) | copy-start | bytes 786436
  7.2 214.2 %all-gather.3.cloned.1.call-start = ((), (), s32[]{:S(2)}) async-start(), calls=%async_computation | async-start | bytes 2228224 | tf_op jit(solution)/shard_map/all_gather | solution.py:98
  8.3 19.8 %collective-permute-start = (bf16[2,128,32]{2,1,0:T(8,128)(2,1)S(1)}, bf16[2,128,32]{2,1,0:T(8,128)(2,1)S(1)}, u32[]{:S(2)}, u32[]{:S(2)}) collective-permute-start(bf16[2,128,32]{2,1,0:T(8,128)(2,1)S(1)} %slice.1061), channel_id=1, source_target_pairs={{0,16},{16,32},{32,48},{48,64},{64,80},{80,96},{96,112},{112,128},... | collective-permute-start | bytes 49160 | tf_op jit(solution)/shard_map/ppermute | solution.py:20
  10.1 18.0 %collective-permute-start.1 = (bf16[2,128,32]{2,1,0:T(8,128)(2,1)S(1)}, bf16[2,128,32]{2,1,0:T(8,128)(2,1)S(1)}, u32[]{:S(2)}, u32[]{:S(2)}) collective-permute-start(bf16[2,128,32]{2,1,0:T(8,128)(2,1)S(1)} %slice.1063), channel_id=1, source_target_pairs={{16,0},{32,16},{48,32},{64,48},{80,64},{96,80},{112,96},{128,112},... | collective-permute-start | bytes 49160 | tf_op jit(solution)/shard_map/ppermute | solution.py:23
  28.4 13.6 %collective-permute-start.2 = (bf16[36,2,32]{1,2,0:T(8,128)(2,1)S(1)}, bf16[36,2,32]{1,2,0:T(8,128)(2,1)S(1)}, u32[]{:S(2)}, u32[]{:S(2)}) collective-permute-start(bf16[36,2,32]{1,2,0:T(8,128)(2,1)S(1)} %get-tuple-element.8), channel_id=1, source_target_pairs={{0,1},{1,2},{2,3},{3,4},{4,5},{5,6},{6,7},{7,8},{8,9},{9,10},{10,1... | collective-permute-start | bytes 13832 | tf_op jit(solution)/shard_map/ppermute | solution.py:20
  31.9 10.3 %collective-permute-start.3 = (bf16[36,2,32]{1,2,0:T(8,128)(2,1)S(1)}, bf16[36,2,32]{1,2,0:T(8,128)(2,1)S(1)}, u32[]{:S(2)}, u32[]{:S(2)}) collective-permute-start(bf16[36,2,32]{1,2,0:T(8,128)(2,1)S(1)} %get-tuple-element.9), channel_id=1, source_target_pairs={{1,0},{2,1},{3,2},{4,3},{5,4},{6,5},{7,6},{8,7},{9,8},{10,9},{11,1... | collective-permute-start | bytes 13832 | tf_op jit(solution)/shard_map/ppermute | solution.py:23
  48.0 5.2 %collective-permute-start.4 = (bf16[1,4096]{1,0:T(2,128)(2,1)S(1)}, bf16[1,4096]{1,0:T(2,128)(2,1)S(1)}, u32[]{:S(2)}, u32[]{:S(2)}) collective-permute-start(bf16[1,4096]{1,0:T(2,128)(2,1)S(1)} %slice.1366), channel_id=1, source_target_pairs={{0,16},{16,32},{32,48},{48,64},{64,80},{80,96},{96,112},{112,128},... | collective-permute-start | bytes 24584 | tf_op jit(solution)/shard_map/ppermute | solution.py:12
  53.8 7.7 %collective-permute-start.5 = (bf16[33,32]{1,0:T(8,128)(2,1)S(1)}, bf16[33,32]{1,0:T(8,128)(2,1)S(1)}, u32[]{:S(2)}, u32[]{:S(2)}) collective-permute-start(bf16[33,32]{1,0:T(8,128)(2,1)S(1)} %fusion.143), channel_id=1, source_target_pairs={{0,1},{1,2},{2,3},{3,4},{4,5},{5,6},{6,7},{7,8},{8,9},{9,10},{10,1... | collective-permute-start | bytes 6344 | tf_op jit(solution)/shard_map/ppermute | solution.py:12
  64.8 5.4 %collective-permute-start.6 = (bf16[1,4096]{1,0:T(2,128)(2,1)S(1)}, bf16[1,4096]{1,0:T(2,128)(2,1)S(1)}, u32[]{:S(2)}, u32[]{:S(2)}) collective-permute-start(bf16[1,4096]{1,0:T(2,128)(2,1)S(1)} %slice.1129), channel_id=1, source_target_pairs={{0,16},{16,32},{32,48},{48,64},{64,80},{80,96},{96,112},{112,128},... | collective-permute-start | bytes 24584 | tf_op jit(solution)/shard_map/ppermute | solution.py:12
  70.5 7.6 %collective-permute-start.7 = (bf16[17,64]{1,0:T(8,128)(2,1)S(1)}, bf16[17,64]{1,0:T(8,128)(2,1)S(1)}, u32[]{:S(2)}, u32[]{:S(2)}) collective-permute-start(bf16[17,64]{1,0:T(8,128)(2,1)S(1)} %fusion.184), channel_id=1, source_target_pairs={{0,1},{1,2},{2,3},{3,4},{4,5},{5,6},{6,7},{7,8},{8,9},{9,10},{10,1... | collective-permute-start | bytes 6536 | tf_op jit(solution)/shard_map/ppermute | solution.py:12
  79.6 4.5 %collective-permute-start.8 = (bf16[1,4096]{1,0:T(2,128)(2,1)S(1)}, bf16[1,4096]{1,0:T(2,128)(2,1)S(1)}, u32[]{:S(2)}, u32[]{:S(2)}) collective-permute-start(bf16[1,4096]{1,0:T(2,128)(2,1)S(1)} %bitcast.639), channel_id=1, source_target_pairs={{0,16},{16,32},{32,48},{48,64},{64,80},{80,96},{96,112},{112,128},... | collective-permute-start | bytes 24584 | tf_op jit(solution)/shard_map/ppermute | solution.py:12
  84.1 7.6 %collective-permute-start.9 = (bf16[9,128]{1,0:T(8,128)(2,1)S(1)}, bf16[9,128]{1,0:T(8,128)(2,1)S(1)}, u32[]{:S(2)}, u32[]{:S(2)}) collective-permute-start(bf16[9,128]{1,0:T(8,128)(2,1)S(1)} %fusion.186), channel_id=1, source_target_pairs={{0,1},{1,2},{2,3},{3,4},{4,5},{5,6},{6,7},{7,8},{8,9},{9,10},{10,1... | collective-permute-start | bytes 6920 | tf_op jit(solution)/shard_map/ppermute | solution.py:12
  86.2 78.8 %copy-start.64 = (f32[1,1,512]{2,0,1:T(1,128)S(1)}, f32[1,1,512]{2,0,1:T(1,128)}, u32[]{:S(2)}) copy-start(f32[1,1,512]{2,0,1:T(1,128)} %get-tuple-element.39) | copy-start | bytes 6148
  86.2 78.9 %copy-start.14 = (f32[4,4,8,128]{3,2,1,0:T(8,128)S(1)}, f32[4,4,8,128]{3,2,1,0:T(8,128)}, u32[]{:S(2)}) copy-start(f32[4,4,8,128]{3,2,1,0:T(8,128)} %broadcast_bitcast_fusion.2) | copy-start | bytes 196612
  86.2 78.8 %copy-start.15 = (f32[4,4,8,128]{3,2,1,0:T(8,128)S(1)}, f32[4,4,8,128]{3,2,1,0:T(8,128)}, u32[]{:S(2)}) copy-start(f32[4,4,8,128]{3,2,1,0:T(8,128)} %broadcast_bitcast_fusion.1) | copy-start | bytes 196612
  91.7 73.4 %copy-start.16 = (f32[4,4,8,128]{3,2,1,0:T(8,128)S(1)}, f32[4,4,8,128]{3,2,1,0:T(8,128)}, u32[]{:S(2)}) copy-start(f32[4,4,8,128]{3,2,1,0:T(8,128)} %broadcast_bitcast_fusion) | copy-start | bytes 196612
  91.8 74.0 %copy-start.17 = (f32[4,4,8,128]{3,2,1,0:T(8,128)S(1)}, f32[4,4,8,128]{3,2,1,0:T(8,128)}, u32[]{:S(2)}) copy-start(f32[4,4,8,128]{3,2,1,0:T(8,128)} %broadcast_bitcast_fusion.8) | copy-start | bytes 196612
  91.9 74.5 %copy-start.18 = (f32[4,4,8,128]{3,2,1,0:T(8,128)S(1)}, f32[4,4,8,128]{3,2,1,0:T(8,128)}, u32[]{:S(2)}) copy-start(f32[4,4,8,128]{3,2,1,0:T(8,128)} %broadcast_bitcast_fusion.7) | copy-start | bytes 196612
  92.0 75.1 %copy-start.19 = (f32[4,4,8,128]{3,2,1,0:T(8,128)S(1)}, f32[4,4,8,128]{3,2,1,0:T(8,128)}, u32[]{:S(2)}) copy-start(f32[4,4,8,128]{3,2,1,0:T(8,128)} %broadcast_bitcast_fusion.6) | copy-start | bytes 196612
  92.0 75.7 %copy-start.20 = (f32[4,4,8,128]{3,2,1,0:T(8,128)S(1)}, f32[4,4,8,128]{3,2,1,0:T(8,128)}, u32[]{:S(2)}) copy-start(f32[4,4,8,128]{3,2,1,0:T(8,128)} %broadcast_bitcast_fusion.5) | copy-start | bytes 196612
  93.1 75.3 %copy-start.21 = (f32[4,4,8,128]{3,2,1,0:T(8,128)S(1)}, f32[4,4,8,128]{3,2,1,0:T(8,128)}, u32[]{:S(2)}) copy-start(f32[4,4,8,128]{3,2,1,0:T(8,128)} %broadcast_bitcast_fusion.4) | copy-start | bytes 196612
  93.1 75.9 %copy-start.22 = (f32[4,4,8,128]{3,2,1,0:T(8,128)S(1)}, f32[4,4,8,128]{3,2,1,0:T(8,128)}, u32[]{:S(2)}) copy-start(f32[4,4,8,128]{3,2,1,0:T(8,128)} %broadcast_bitcast_fusion.3) | copy-start | bytes 196612
  93.4 5.1 %collective-permute-start.10 = (bf16[1,4096]{1,0:T(2,128)(2,1)S(1)}, bf16[1,4096]{1,0:T(2,128)(2,1)S(1)}, u32[]{:S(2)}, u32[]{:S(2)}) collective-permute-start(bf16[1,4096]{1,0:T(2,128)(2,1)S(1)} %bitcast.640), channel_id=1, source_target_pairs={{0,16},{16,32},{32,48},{48,64},{64,80},{80,96},{96,112},{112,128},... | collective-permute-start | bytes 24584 | tf_op jit(solution)/shard_map/ppermute | solution.py:12
  97.7 72.6 %copy-start.63 = (f32[1,1,512]{2,0,1:T(1,128)S(1)}, f32[1,1,512]{2,0,1:T(1,128)}, u32[]{:S(2)}) copy-start(f32[1,1,512]{2,0,1:T(1,128)} %get-tuple-element.38) | copy-start | bytes 6148
  97.7 73.2 %copy-start.62 = (f32[1,1,512]{2,0,1:T(1,128)S(1)}, f32[1,1,512]{2,0,1:T(1,128)}, u32[]{:S(2)}) copy-start(f32[1,1,512]{2,0,1:T(1,128)} %get-tuple-element.37) | copy-start | bytes 6148
  98.6 73.0 %copy-start.61 = (f32[1,1,512]{2,0,1:T(1,128)S(1)}, f32[1,1,512]{2,0,1:T(1,128)}, u32[]{:S(2)}) copy-start(f32[1,1,512]{2,0,1:T(1,128)} %get-tuple-element.36) | copy-start | bytes 6148
  98.6 7.6 %collective-permute-start.11 = (bf16[5,256]{1,0:T(8,128)(2,1)S(1)}, bf16[5,256]{1,0:T(8,128)(2,1)S(1)}, u32[]{:S(2)}, u32[]{:S(2)}) collective-permute-start(bf16[5,256]{1,0:T(8,128)(2,1)S(1)} %fusion.185), channel_id=1, source_target_pairs={{0,1},{1,2},{2,3},{3,4},{4,5},{5,6},{6,7},{7,8},{8,9},{9,10},{10,1... | collective-permute-start | bytes 7688 | tf_op jit(solution)/shard_map/ppermute | solution.py:12
  100.6 71.6 %copy-start.60 = (f32[1,1,512]{2,0,1:T(1,128)S(1)}, f32[1,1,512]{2,0,1:T(1,128)}, u32[]{:S(2)}) copy-start(f32[1,1,512]{2,0,1:T(1,128)} %get-tuple-element.35) | copy-start | bytes 6148
  106.7 68.6 %copy-start.54 = (f32[1,1,512]{2,0,1:T(1,128)S(1)}, f32[1,1,512]{2,0,1:T(1,128)}, u32[]{:S(2)}) copy-start(f32[1,1,512]{2,0,1:T(1,128)} %get-tuple-element.30) | copy-start | bytes 6148
  106.8 69.2 %copy-start.53 = (f32[1,1,512]{2,0,1:T(1,128)S(1)}, f32[1,1,512]{2,0,1:T(1,128)}, u32[]{:S(2)}) copy-start(f32[1,1,512]{2,0,1:T(1,128)} %get-tuple-element.29) | copy-start | bytes 6148
  106.8 5.1 %collective-permute-start.12 = (bf16[1,4096]{1,0:T(2,128)(2,1)S(1)}, bf16[1,4096]{1,0:T(2,128)(2,1)S(1)}, u32[]{:S(2)}, u32[]{:S(2)}) collective-permute-start(bf16[1,4096]{1,0:T(2,128)(2,1)S(1)} %bitcast.638), channel_id=1, source_target_pairs={{0,16},{16,32},{32,48},{48,64},{64,80},{80,96},{96,112},{112,128},... | collective-permute-start | bytes 24584 | tf_op jit(solution)/shard_map/ppermute | solution.py:12
  111.9 7.6 %collective-permute-start.13 = (bf16[3,512]{1,0:T(4,128)(2,1)S(1)}, bf16[3,512]{1,0:T(4,128)(2,1)S(1)}, u32[]{:S(2)}, u32[]{:S(2)}) collective-permute-start(bf16[3,512]{1,0:T(4,128)(2,1)S(1)} %pad_maximum_fusion.6), channel_id=1, source_target_pairs={{0,1},{1,2},{2,3},{3,4},{4,5},{5,6},{6,7},{7,8},{8,9},{9,10},{10,1... | collective-permute-start | bytes 9224 | tf_op jit(solution)/shard_map/ppermute | solution.py:12
  (76 other events, 1632.9 us)
Sparse Core Ops, SparseCore 0:
  165.1 56.1 all-gather.2
where the time goes:
time: 280 us; the launch traced here: 279 us
  local copies, waits for them, and re-layouts  93.6 us (33%)
  waiting for transfers between devices  69.5 us (25%)
  blocking collectives  43.3 us (15%)
  starting transfers between devices  42.3 us (15%)
  between operations  16.7 us (6%)
  matrix products  7.75 us (3%)
  other arithmetic  5.42 us (2%)
    all_gather x1, blocking collectives, local(): hidden = lax.all_gather(hidden, 'gx', axis=0, tiled=True)  43.3 us
    all_gather x1, waiting for transfers between devices, local(): hidden = lax.all_gather(hidden, 'gy', axis=1, tiled=True)  41.1 us
    unnamed x313, local copies, waits for them, and re-layouts  37.7 us
    ppermute x10, starting transfers between devices, shifted(): lax.ppermute(value, axis, [(source, source + steps) for source in range(l...  31.2 us
    slice x22, local copies, waits for them, and re-layouts, down_level(): slab = extended[first:first + rows:2]  29.2 us
    ppermute x10, waiting for transfers between devices, shifted(): lax.ppermute(value, axis, [(source, source + steps) for source in range(l...  28.3 us
    slice x6, local copies, waits for them, and re-layouts, down_level(): total = total + piece.astype(jnp.float32) * tiled[3 * first + second]  8.45 us
    dot_general x9, matrix products, point_flat(): mixed = jnp.dot(flat, weight, preferred_element_type=jnp.float32)  7.75 us
  transfers between devices with their start and end apart: 15, of which 11 were waited for; matrix products, arithmetic and copies ran while one was open for 15% of the time, Pallas kernels for 0%

commit v1 on v0

--- a/solution.py
+++ b/solution.py
@@ -94,7 +94,9 @@
         ):
             hidden = down_level(hidden, dwc[level], pwc[level], True, True)
             finished = level + 1
-    hidden = lax.all_gather(hidden, "gx", axis=0, tiled=True)
+    hidden = jnp.concatenate(
+        lax.all_to_all(jnp.stack([hidden] * lax.axis_size("gx")), "gx", 0, 0), axis=0
+    )
     hidden = lax.all_gather(hidden, "gy", axis=1, tiled=True)
     for level in range(finished, LC):
         hidden = down_level(hidden, dwc[level], pwc[level], False, False)

time: 280 us -> 269 us (0.961)
  blocking collectives: 43.3 us -> 0 us
  starting transfers between devices: 42.3 us -> 67.5 us
  waiting for transfers between devices: 69.5 us -> 78.9 us
  local copies, waits for them, and re-layouts: 93.6 us -> 90.7 us
    all_gather x1 -> x0, blocking collectives: 43.3 us -> none  [local(): hidden = lax.all_gather(hidden, 'gx', axis=0, tiled=True)]
    all_to_all x0 -> x1, starting transfers between devices: none -> 25.3 us  [local(): lax.all_to_all(jnp.stack([hidden] * lax.axis_size('gx')), 'gx', 0, 0)]
    all_to_all x0 -> x1, waiting for transfers between devices: none -> 17.1 us  [local(): lax.all_to_all(jnp.stack([hidden] * lax.axis_size('gx')), 'gx', 0, 0)]
    all_gather x1, waiting for transfers between devices: 41.1 us -> 33.4 us  [local(): hidden = lax.all_gather(hidden, 'gy', axis=1, tiled=True)]
    unnamed x313 -> x318, local copies, waits for them, and re-layouts: 37.7 us -> 30 us
    slice x22, local copies, waits for them, and re-layouts: 29.2 us -> 33.4 us  [down_level(): slab = extended[first:first + rows:2]]
  transfers between devices with their start and end apart: 15 -> 16, of which waited for: 11 -> 12; matrix products, arithmetic and copies ran while one was open for 15% -> 14% of each run, Pallas kernels for 0% -> 0%
where the time goes in v1:
time: 269 us; the launch traced here: 268 us
  local copies, waits for them, and re-layouts  90.7 us (34%)
  waiting for transfers between devices  78.9 us (29%)
  starting transfers between devices  67.5 us (25%)
  between operations  16.8 us (6%)
  matrix products  6.87 us (3%)
  other arithmetic  6.79 us (3%)
    slice x22, local copies, waits for them, and re-layouts, down_level(): slab = extended[first:first + rows:2]  33.4 us
    all_gather x1, waiting for transfers between devices, local(): hidden = lax.all_gather(hidden, 'gy', axis=1, tiled=True)  33.4 us
    ppermute x10, starting transfers between devices, shifted(): lax.ppermute(value, axis, [(source, source + steps) for source in range(l...  31.2 us
    unnamed x318, local copies, waits for them, and re-layouts  30 us
    ppermute x10, waiting for transfers between devices, shifted(): lax.ppermute(value, axis, [(source, source + steps) for source in range(l...  28.3 us
    all_to_all x1, starting transfers between devices, local(): lax.all_to_all(jnp.stack([hidden] * lax.axis_size('gx')), 'gx', 0, 0)  25.3 us
    all_to_all x1, waiting for transfers between devices, local(): lax.all_to_all(jnp.stack([hidden] * lax.axis_size('gx')), 'gx', 0, 0)  17.1 us
    slice x6, local copies, waits for them, and re-layouts, down_level(): total = total + piece.astype(jnp.float32) * tiled[3 * first + second]  8.43 us
  transfers between devices with their start and end apart: 16, of which 12 were waited for; matrix products, arithmetic and copies ran while one was open for 14% of the time, Pallas kernels for 0%

profile of v1, /device:TPU:2, one launch (start us, length us, event | category | flops | bytes accessed | tf_op | source)
XLA Modules:
  0.0 267.6 jit_solution(15902615705908386746)
XLA Ops:
  8.2 1.7 collective-permute-start
  11.4 1.5 fusion.199
  12.9 1.5 fusion.198
  15.4 1.6 slice_bitcast_fusion.43
  17.0 1.6 fusion.204
  22.5 1.6 slice_bitcast_fusion.34
  24.1 1.7 reshape.1237
  26.6 3.5 %collective-permute-start.2 = (bf16[36,2,32]{1,2,0:T(8,128)(2,1)S(1)}, bf16[36,2,32]{1,2,0:T(8,128)(2,1)S(1)}, u32[]{:S(2)}, u32[]{:S(2)}) collective-permute-start(bf16[36,2,32]{1,2,0:T(8,128)(2,1)S(1)} %get-tuple-element.8), channel_id=1, source_target_pairs={{0,1},{1,2},{2,3},{3,4},{4,5},{5,6},{6,7},{7,8},{8,9},{9,10},{10,1... | collective-permute-start | bytes 13832 | tf_op jit(solution)/shard_map/ppermute | solution.py:20
  30.1 4.5 %collective-permute-start.3 = (bf16[36,2,32]{1,2,0:T(8,128)(2,1)S(1)}, bf16[36,2,32]{1,2,0:T(8,128)(2,1)S(1)}, u32[]{:S(2)}, u32[]{:S(2)}) collective-permute-start(bf16[36,2,32]{1,2,0:T(8,128)(2,1)S(1)} %get-tuple-element.9), channel_id=1, source_target_pairs={{1,0},{2,1},{3,2},{4,3},{5,4},{6,5},{7,6},{8,7},{9,8},{10,9},{11,1... | collective-permute-start | bytes 13832 | tf_op jit(solution)/shard_map/ppermute | solution.py:23
  46.2 4.0 %collective-permute-start.4 = (bf16[1,4096]{1,0:T(2,128)(2,1)S(1)}, bf16[1,4096]{1,0:T(2,128)(2,1)S(1)}, u32[]{:S(2)}, u32[]{:S(2)}) collective-permute-start(bf16[1,4096]{1,0:T(2,128)(2,1)S(1)} %slice.1366), channel_id=1, source_target_pairs={{0,16},{16,32},{32,48},{48,64},{64,80},{80,96},{96,112},{112,128},... | collective-permute-start | bytes 24584 | tf_op jit(solution)/shard_map/ppermute | solution.py:12
  52.0 2.7 collective-permute-start.5
  55.5 4.2 %collective-permute-done.5 = bf16[33,32]{1,0:T(8,128)(2,1)S(1)} collective-permute-done((bf16[33,32]{1,0:T(8,128)(2,1)S(1)}, bf16[33,32]{1,0:T(8,128)(2,1)S(1)}, u32[]{:S(2)}, u32[]{:S(2)}) %collective-permute-start.5) | collective-permute-done | bytes 2144 | tf_op jit(solution)/shard_map/ppermute | solution.py:12
  63.0 4.7 %collective-permute-start.6 = (bf16[1,4096]{1,0:T(2,128)(2,1)S(1)}, bf16[1,4096]{1,0:T(2,128)(2,1)S(1)}, u32[]{:S(2)}, u32[]{:S(2)}) collective-permute-start(bf16[1,4096]{1,0:T(2,128)(2,1)S(1)} %slice.1129), channel_id=1, source_target_pairs={{0,16},{16,32},{32,48},{48,64},{64,80},{80,96},{96,112},{112,128},... | collective-permute-start | bytes 24584 | tf_op jit(solution)/shard_map/ppermute | solution.py:12
  68.7 1.9 collective-permute-start.7
  70.9 5.3 %collective-permute-done.7 = bf16[17,64]{1,0:T(8,128)(2,1)S(1)} collective-permute-done((bf16[17,64]{1,0:T(8,128)(2,1)S(1)}, bf16[17,64]{1,0:T(8,128)(2,1)S(1)}, u32[]{:S(2)}, u32[]{:S(2)}) %collective-permute-start.7) | collective-permute-done | bytes 2208 | tf_op jit(solution)/shard_map/ppermute | solution.py:12
  77.8 3.7 %collective-permute-start.8 = (bf16[1,4096]{1,0:T(2,128)(2,1)S(1)}, bf16[1,4096]{1,0:T(2,128)(2,1)S(1)}, u32[]{:S(2)}, u32[]{:S(2)}) collective-permute-start(bf16[1,4096]{1,0:T(2,128)(2,1)S(1)} %bitcast.645), channel_id=1, source_target_pairs={{0,16},{16,32},{32,48},{48,64},{64,80},{80,96},{96,112},{112,128},... | collective-permute-start | bytes 24584 | tf_op jit(solution)/shard_map/ppermute | solution.py:12
  82.3 1.9 collective-permute-start.9
  84.4 5.5 %collective-permute-done.9 = bf16[9,128]{1,0:T(8,128)(2,1)S(1)} collective-permute-done((bf16[9,128]{1,0:T(8,128)(2,1)S(1)}, bf16[9,128]{1,0:T(8,128)(2,1)S(1)}, u32[]{:S(2)}, u32[]{:S(2)}) %collective-permute-start.9) | collective-permute-done | bytes 2336 | tf_op jit(solution)/shard_map/ppermute | solution.py:12
  90.7 4.2 %collective-permute-start.10 = (bf16[1,4096]{1,0:T(2,128)(2,1)S(1)}, bf16[1,4096]{1,0:T(2,128)(2,1)S(1)}, u32[]{:S(2)}, u32[]{:S(2)}) collective-permute-start(bf16[1,4096]{1,0:T(2,128)(2,1)S(1)} %bitcast.646), channel_id=1, source_target_pairs={{0,16},{16,32},{32,48},{48,64},{64,80},{80,96},{96,112},{112,128},... | collective-permute-start | bytes 24584 | tf_op jit(solution)/shard_map/ppermute | solution.py:12
  95.9 1.9 collective-permute-start.11
  97.9 5.6 %collective-permute-done.11 = bf16[5,256]{1,0:T(8,128)(2,1)S(1)} collective-permute-done((bf16[5,256]{1,0:T(8,128)(2,1)S(1)}, bf16[5,256]{1,0:T(8,128)(2,1)S(1)}, u32[]{:S(2)}, u32[]{:S(2)}) %collective-permute-start.11) | collective-permute-done | bytes 2592 | tf_op jit(solution)/shard_map/ppermute | solution.py:12
  104.1 4.2 %collective-permute-start.12 = (bf16[1,4096]{1,0:T(2,128)(2,1)S(1)}, bf16[1,4096]{1,0:T(2,128)(2,1)S(1)}, u32[]{:S(2)}, u32[]{:S(2)}) collective-permute-start(bf16[1,4096]{1,0:T(2,128)(2,1)S(1)} %bitcast.644), channel_id=1, source_target_pairs={{0,16},{16,32},{32,48},{48,64},{64,80},{80,96},{96,112},{112,128},... | collective-permute-start | bytes 24584 | tf_op jit(solution)/shard_map/ppermute | solution.py:12
  109.1 1.9 collective-permute-start.13
  111.2 5.6 %collective-permute-done.13 = bf16[3,512]{1,0:T(4,128)(2,1)S(1)} collective-permute-done((bf16[3,512]{1,0:T(4,128)(2,1)S(1)}, bf16[3,512]{1,0:T(4,128)(2,1)S(1)}, u32[]{:S(2)}, u32[]{:S(2)}) %collective-permute-start.13) | collective-permute-done | bytes 3104 | tf_op jit(solution)/shard_map/ppermute | solution.py:12
  121.1 25.3 %all-to-all-start = ((bf16[32,2,1024]{2,1,0:T(2,128)(2,1)}), bf16[32,2,1024]{2,1,0:T(2,128)(2,1)S(1)}, u32[]{:S(2)}, u32[]{:S(2)}) async-start(bf16[32,2,1024]{2,1,0:T(2,128)(2,1)} %reshape.1344), calls=%async_computation | async-start | bytes 262144 | tf_op jit(solution)/shard_map/all_to_all | solution.py:98
  146.5 17.1 %all-to-all-done = bf16[32,2,1024]{2,1,0:T(2,128)(2,1)S(1)} async-done(((bf16[32,2,1024]{2,1,0:T(2,128)(2,1)}), bf16[32,2,1024]{2,1,0:T(2,128)(2,1)S(1)}, u32[]{:S(2)}, u32[]{:S(2)}) %all-to-all-start) | async-done | bytes 131104 | tf_op jit(solution)/shard_map/all_to_all | solution.py:98
  179.7 33.4 %all-gather.3.cloned.1.call-done = bf16[32,1,32768]{2,0,1:T(8,128)(2,1)} async-done(((bf16[32,1,2048]{2,0,1:T(8,128)(2,1)}), bf16[32,1,32768]{2,0,1:T(8,128)(2,1)}) %all-gather.3.cloned.1.call-update) | async-done | bytes 2097168 | tf_op jit(solution)/shard_map/all_gather | solution.py:100
  213.1 11.4 %slice.1272 = bf16[16,32768]{1,0:T(8,128)(2,1)} slice(bf16[32,32768]{1,0:T(8,128)(2,1)} %bitcast.511), slice={[0:32:2], [0:32768:1]} | slice | bytes 2097152 | tf_op jit(solution)/shard_map/slice | solution.py:57
  224.5 4.6 %slice.1282 = bf16[16,32768]{1,0:T(8,128)(2,1)S(1)} slice(bf16[32,32768]{1,0:T(8,128)(2,1)S(1)} %bitcast.512), slice={[1:32:2], [0:32768:1]} | slice | bytes 2097152 | tf_op jit(solution)/shard_map/slice | solution.py:57
  229.1 1.8 concatenate.136
  231.0 10.6 %slice.1262 = bf16[16,32768]{1,0:T(8,128)(2,1)S(1)} slice(bf16[33,32768]{1,0:T(8,128)(2,1)} %concatenate.136), slice={[0:32:2], [0:32768:1]} | slice | bytes 2097152 | tf_op jit(solution)/shard_map/slice | solution.py:57
  248.5 1.7 fusion.7
  (515 shorter events, 68.3 us)
Async XLA Ops:
  7.2 96.6 %copy-start = (bf16[256,512]{1,0:T(8,128)(2,1)S(1)}, bf16[256,512]{1,0:T(8,128)(2,1)}, u32[]{:S(2)}) copy-start(bf16[256,512]{1,0:T(8,128)(2,1)} %param.23) | copy-start | bytes 786436
  8.2 18.0 %collective-permute-start = (bf16[2,128,32]{2,1,0:T(8,128)(2,1)S(1)}, bf16[2,128,32]{2,1,0:T(8,128)(2,1)S(1)}, u32[]{:S(2)}, u32[]{:S(2)}) collective-permute-start(bf16[2,128,32]{2,1,0:T(8,128)(2,1)S(1)} %slice.1061), channel_id=1, source_target_pairs={{0,16},{16,32},{32,48},{48,64},{64,80},{80,96},{96,112},{112,128},... | collective-permute-start | bytes 49160 | tf_op jit(solution)/shard_map/ppermute | solution.py:20
  10.1 16.2 %collective-permute-start.1 = (bf16[2,128,32]{2,1,0:T(8,128)(2,1)S(1)}, bf16[2,128,32]{2,1,0:T(8,128)(2,1)S(1)}, u32[]{:S(2)}, u32[]{:S(2)}) collective-permute-start(bf16[2,128,32]{2,1,0:T(8,128)(2,1)S(1)} %slice.1063), channel_id=1, source_target_pairs={{16,0},{32,16},{48,32},{64,48},{80,64},{96,80},{112,96},{128,112},... | collective-permute-start | bytes 49160 | tf_op jit(solution)/shard_map/ppermute | solution.py:23
  26.6 13.6 %collective-permute-start.2 = (bf16[36,2,32]{1,2,0:T(8,128)(2,1)S(1)}, bf16[36,2,32]{1,2,0:T(8,128)(2,1)S(1)}, u32[]{:S(2)}, u32[]{:S(2)}) collective-permute-start(bf16[36,2,32]{1,2,0:T(8,128)(2,1)S(1)} %get-tuple-element.8), channel_id=1, source_target_pairs={{0,1},{1,2},{2,3},{3,4},{4,5},{5,6},{6,7},{7,8},{8,9},{9,10},{10,1... | collective-permute-start | bytes 13832 | tf_op jit(solution)/shard_map/ppermute | solution.py:20
  30.1 10.3 %collective-permute-start.3 = (bf16[36,2,32]{1,2,0:T(8,128)(2,1)S(1)}, bf16[36,2,32]{1,2,0:T(8,128)(2,1)S(1)}, u32[]{:S(2)}, u32[]{:S(2)}) collective-permute-start(bf16[36,2,32]{1,2,0:T(8,128)(2,1)S(1)} %get-tuple-element.9), channel_id=1, source_target_pairs={{1,0},{2,1},{3,2},{4,3},{5,4},{6,5},{7,6},{8,7},{9,8},{10,9},{11,1... | collective-permute-start | bytes 13832 | tf_op jit(solution)/shard_map/ppermute | solution.py:23
  46.2 5.2 %collective-permute-start.4 = (bf16[1,4096]{1,0:T(2,128)(2,1)S(1)}, bf16[1,4096]{1,0:T(2,128)(2,1)S(1)}, u32[]{:S(2)}, u32[]{:S(2)}) collective-permute-start(bf16[1,4096]{1,0:T(2,128)(2,1)S(1)} %slice.1366), channel_id=1, source_target_pairs={{0,16},{16,32},{32,48},{48,64},{64,80},{80,96},{96,112},{112,128},... | collective-permute-start | bytes 24584 | tf_op jit(solution)/shard_map/ppermute | solution.py:12
  52.0 7.7 %collective-permute-start.5 = (bf16[33,32]{1,0:T(8,128)(2,1)S(1)}, bf16[33,32]{1,0:T(8,128)(2,1)S(1)}, u32[]{:S(2)}, u32[]{:S(2)}) collective-permute-start(bf16[33,32]{1,0:T(8,128)(2,1)S(1)} %fusion.143), channel_id=1, source_target_pairs={{0,1},{1,2},{2,3},{3,4},{4,5},{5,6},{6,7},{7,8},{8,9},{9,10},{10,1... | collective-permute-start | bytes 6344 | tf_op jit(solution)/shard_map/ppermute | solution.py:12
  63.0 5.4 %collective-permute-start.6 = (bf16[1,4096]{1,0:T(2,128)(2,1)S(1)}, bf16[1,4096]{1,0:T(2,128)(2,1)S(1)}, u32[]{:S(2)}, u32[]{:S(2)}) collective-permute-start(bf16[1,4096]{1,0:T(2,128)(2,1)S(1)} %slice.1129), channel_id=1, source_target_pairs={{0,16},{16,32},{32,48},{48,64},{64,80},{80,96},{96,112},{112,128},... | collective-permute-start | bytes 24584 | tf_op jit(solution)/shard_map/ppermute | solution.py:12
  68.7 7.6 %collective-permute-start.7 = (bf16[17,64]{1,0:T(8,128)(2,1)S(1)}, bf16[17,64]{1,0:T(8,128)(2,1)S(1)}, u32[]{:S(2)}, u32[]{:S(2)}) collective-permute-start(bf16[17,64]{1,0:T(8,128)(2,1)S(1)} %fusion.187), channel_id=1, source_target_pairs={{0,1},{1,2},{2,3},{3,4},{4,5},{5,6},{6,7},{7,8},{8,9},{9,10},{10,1... | collective-permute-start | bytes 6536 | tf_op jit(solution)/shard_map/ppermute | solution.py:12
  77.8 4.5 %collective-permute-start.8 = (bf16[1,4096]{1,0:T(2,128)(2,1)S(1)}, bf16[1,4096]{1,0:T(2,128)(2,1)S(1)}, u32[]{:S(2)}, u32[]{:S(2)}) collective-permute-start(bf16[1,4096]{1,0:T(2,128)(2,1)S(1)} %bitcast.645), channel_id=1, source_target_pairs={{0,16},{16,32},{32,48},{48,64},{64,80},{80,96},{96,112},{112,128},... | collective-permute-start | bytes 24584 | tf_op jit(solution)/shard_map/ppermute | solution.py:12
  82.3 7.6 %collective-permute-start.9 = (bf16[9,128]{1,0:T(8,128)(2,1)S(1)}, bf16[9,128]{1,0:T(8,128)(2,1)S(1)}, u32[]{:S(2)}, u32[]{:S(2)}) collective-permute-start(bf16[9,128]{1,0:T(8,128)(2,1)S(1)} %fusion.189), channel_id=1, source_target_pairs={{0,1},{1,2},{2,3},{3,4},{4,5},{5,6},{6,7},{7,8},{8,9},{9,10},{10,1... | collective-permute-start | bytes 6920 | tf_op jit(solution)/shard_map/ppermute | solution.py:12
  90.0 56.5 %copy-start.62 = (f32[1,1,512]{2,0,1:T(1,128)S(1)}, f32[1,1,512]{2,0,1:T(1,128)}, u32[]{:S(2)}) copy-start(f32[1,1,512]{2,0,1:T(1,128)} %get-tuple-element.46) | copy-start | bytes 6148
  90.0 56.5 %copy-start.61 = (f32[1,1,512]{2,0,1:T(1,128)S(1)}, f32[1,1,512]{2,0,1:T(1,128)}, u32[]{:S(2)}) copy-start(f32[1,1,512]{2,0,1:T(1,128)} %get-tuple-element.45) | copy-start | bytes 6148
  90.7 5.1 %collective-permute-start.10 = (bf16[1,4096]{1,0:T(2,128)(2,1)S(1)}, bf16[1,4096]{1,0:T(2,128)(2,1)S(1)}, u32[]{:S(2)}, u32[]{:S(2)}) collective-permute-start(bf16[1,4096]{1,0:T(2,128)(2,1)S(1)} %bitcast.646), channel_id=1, source_target_pairs={{0,16},{16,32},{32,48},{48,64},{64,80},{80,96},{96,112},{112,128},... | collective-permute-start | bytes 24584 | tf_op jit(solution)/shard_map/ppermute | solution.py:12
  95.9 68.6 %copy-start.59 = (f32[1,1,512]{2,0,1:T(1,128)S(1)}, f32[1,1,512]{2,0,1:T(1,128)}, u32[]{:S(2)}) copy-start(f32[1,1,512]{2,0,1:T(1,128)} %get-tuple-element.39) | copy-start | bytes 6148
  95.9 68.6 %copy-start.12 = (f32[4,4,8,128]{3,2,1,0:T(8,128)S(1)}, f32[4,4,8,128]{3,2,1,0:T(8,128)}, u32[]{:S(2)}) copy-start(f32[4,4,8,128]{3,2,1,0:T(8,128)} %broadcast_bitcast_fusion.2) | copy-start | bytes 196612
  95.9 7.6 %collective-permute-start.11 = (bf16[5,256]{1,0:T(8,128)(2,1)S(1)}, bf16[5,256]{1,0:T(8,128)(2,1)S(1)}, u32[]{:S(2)}, u32[]{:S(2)}) collective-permute-start(bf16[5,256]{1,0:T(8,128)(2,1)S(1)} %fusion.188), channel_id=1, source_target_pairs={{0,1},{1,2},{2,3},{3,4},{4,5},{5,6},{6,7},{7,8},{8,9},{9,10},{10,1... | collective-permute-start | bytes 7688 | tf_op jit(solution)/shard_map/ppermute | solution.py:12
  103.6 60.9 %copy-start.13 = (f32[4,4,8,128]{3,2,1,0:T(8,128)S(1)}, f32[4,4,8,128]{3,2,1,0:T(8,128)}, u32[]{:S(2)}) copy-start(f32[4,4,8,128]{3,2,1,0:T(8,128)} %broadcast_bitcast_fusion.1) | copy-start | bytes 196612
  103.7 60.8 %copy-start.14 = (f32[4,4,8,128]{3,2,1,0:T(8,128)S(1)}, f32[4,4,8,128]{3,2,1,0:T(8,128)}, u32[]{:S(2)}) copy-start(f32[4,4,8,128]{3,2,1,0:T(8,128)} %broadcast_bitcast_fusion) | copy-start | bytes 196612
  103.8 61.4 %copy-start.15 = (f32[4,4,8,128]{3,2,1,0:T(8,128)S(1)}, f32[4,4,8,128]{3,2,1,0:T(8,128)}, u32[]{:S(2)}) copy-start(f32[4,4,8,128]{3,2,1,0:T(8,128)} %broadcast_bitcast_fusion.8) | copy-start | bytes 196612
  104.0 61.8 %copy-start.16 = (f32[4,4,8,128]{3,2,1,0:T(8,128)S(1)}, f32[4,4,8,128]{3,2,1,0:T(8,128)}, u32[]{:S(2)}) copy-start(f32[4,4,8,128]{3,2,1,0:T(8,128)} %broadcast_bitcast_fusion.7) | copy-start | bytes 196612
  104.0 62.5 %copy-start.17 = (f32[4,4,8,128]{3,2,1,0:T(8,128)S(1)}, f32[4,4,8,128]{3,2,1,0:T(8,128)}, u32[]{:S(2)}) copy-start(f32[4,4,8,128]{3,2,1,0:T(8,128)} %broadcast_bitcast_fusion.6) | copy-start | bytes 196612
  104.1 5.1 %collective-permute-start.12 = (bf16[1,4096]{1,0:T(2,128)(2,1)S(1)}, bf16[1,4096]{1,0:T(2,128)(2,1)S(1)}, u32[]{:S(2)}, u32[]{:S(2)}) collective-permute-start(bf16[1,4096]{1,0:T(2,128)(2,1)S(1)} %bitcast.644), channel_id=1, source_target_pairs={{0,16},{16,32},{32,48},{48,64},{64,80},{80,96},{96,112},{112,128},... | collective-permute-start | bytes 24584 | tf_op jit(solution)/shard_map/ppermute | solution.py:12
  109.1 7.6 %collective-permute-start.13 = (bf16[3,512]{1,0:T(4,128)(2,1)S(1)}, bf16[3,512]{1,0:T(4,128)(2,1)S(1)}, u32[]{:S(2)}, u32[]{:S(2)}) collective-permute-start(bf16[3,512]{1,0:T(4,128)(2,1)S(1)} %pad_maximum_fusion.6), channel_id=1, source_target_pairs={{0,1},{1,2},{2,3},{3,4},{4,5},{5,6},{6,7},{7,8},{8,9},{9,10},{10,1... | collective-permute-start | bytes 9224 | tf_op jit(solution)/shard_map/ppermute | solution.py:12
  119.0 56.4 %copy-start.48 = (f32[1,1,512]{2,0,1:T(1,128)S(1)}, f32[1,1,512]{2,0,1:T(1,128)}, u32[]{:S(2)}) copy-start(f32[1,1,512]{2,0,1:T(1,128)} %get-tuple-element.29) | copy-start | bytes 6148
  119.0 57.0 %copy-start.47 = (f32[1,1,512]{2,0,1:T(1,128)S(1)}, f32[1,1,512]{2,0,1:T(1,128)}, u32[]{:S(2)}) copy-start(f32[1,1,512]{2,0,1:T(1,128)} %get-tuple-element.28) | copy-start | bytes 6148
  120.4 56.9 %copy-start.45 = (f32[1,1,512]{2,0,1:T(1,128)S(1)}, f32[1,1,512]{2,0,1:T(1,128)}, u32[]{:S(2)}) copy-start(f32[1,1,512]{2,0,1:T(1,128)} %get-tuple-element.26) | copy-start | bytes 6148
  120.4 57.5 %copy-start.44 = (f32[1,1,512]{2,0,1:T(1,128)S(1)}, f32[1,1,512]{2,0,1:T(1,128)}, u32[]{:S(2)}) copy-start(f32[1,1,512]{2,0,1:T(1,128)} %get-tuple-element.25) | copy-start | bytes 6148
  120.4 58.1 %copy-start.43 = (f32[1,1,512]{2,0,1:T(1,128)S(1)}, f32[1,1,512]{2,0,1:T(1,128)}, u32[]{:S(2)}) copy-start(f32[1,1,512]{2,0,1:T(1,128)} %get-tuple-element.43) | copy-start | bytes 6148
  120.4 58.7 %copy-start.42 = (f32[1,1,512]{2,0,1:T(1,128)S(1)}, f32[1,1,512]{2,0,1:T(1,128)}, u32[]{:S(2)}) copy-start(f32[1,1,512]{2,0,1:T(1,128)} %get-tuple-element.59) | copy-start | bytes 6148
  121.1 42.5 %all-to-all-start = ((bf16[32,2,1024]{2,1,0:T(2,128)(2,1)}), bf16[32,2,1024]{2,1,0:T(2,128)(2,1)S(1)}, u32[]{:S(2)}, u32[]{:S(2)}) async-start(bf16[32,2,1024]{2,1,0:T(2,128)(2,1)} %reshape.1344), calls=%async_computation | async-start | bytes 262144 | tf_op jit(solution)/shard_map/all_to_all | solution.py:98
  146.4 66.7 %all-gather.3.cloned.1.call-start = ((), (), s32[]{:S(2)}) async-start(), calls=%async_computation.1 | async-start | bytes 2228224 | tf_op jit(solution)/shard_map/all_gather | solution.py:100
  (79 other events, 1618.3 us)
Sparse Core Ops, SparseCore 0:
  164.6 48.4 all-gather.2
